TPU v7x, 32 devices: a whole 2x2x4 slice. The times are simulated.
32 devices in a mesh: dp: 4 (over y, x), ctx: 8 (over z, core).
Axes of the slice: x: 2, y: 2, z: 4, core: 2. Of those that a mesh axis runs over, the one named last changes fastest.
Arguments:
- clip_tokens: bfloat16 [4, 2048, 3072], P('dp', 'ctx'), may hold values from -6 to 6
- qkv_weight: bfloat16 [3, 3072, 1536], P(None, None, 'dp'), may hold values from -0.15625 to 0.15625
- out_weight: bfloat16 [1536, 3072], P('dp'), may hold values from -0.5 to 0.5
- neighbours: int32 [32, 10], P('ctx'), may hold values from 0 to 31, as said below
- counts: int32 [32], P('ctx'), may hold values from 2 to 10, as said below
- bias_index: int32 [32, 10], P('ctx'), may hold values from 0 to 342
- rel_bias: float32 [12, 343], P('dp'), may hold values from -4 to 262
Outputs:
- layer_out: bfloat16 [4, 2048, 3072], P('dp', 'ctx')
Inputs may be any that keep to these rules, and one draw needn't show every extreme that they name: `neighbours`: tile g lies on ctx index g / 4. Row g starts with g itself; its first counts[g] entries are distinct tiles on ctx indices at most 6 away from that of g; the entries from counts[g] on equal g. Of the tiles of one ctx index, those named in the live entries of the rows of another index are at most 2, and exactly 2 for some pairs of indices. `counts`: some tile has 10 live slots.
All inputs are finite; a program needn't handle non-finite values.
Results may differ from a plain program's by a relative error of at most 0.012.
Values may be sent and summed in bfloat16 or wider, within the bound.
No kernel may reach another device: no remote copies, remote signals or barrier semaphores. Data moves between devices by JAX's collectives and lax.ppermute only.
A program may use at most 128 MiB of HBM per device.

v0:
```python
import math
import jax
import jax.numpy as jnp
from jax import lax
from jax.sharding import PartitionSpec as P

TILE = 64
REACH = 6
KMAX = 10


def shifted(value, axis, steps):
    count = lax.axis_size(axis)
    first, last = (max(0, -steps), min(count, count - steps))
    return lax.ppermute(value, axis, [(source, source + steps) for source in range(first, last)])


def local(clip_tokens, qkv_weight, out_weight, neighbours, counts, bias_index, rel_bias):
    heads_here = rel_bias.shape[0]
    width_here = out_weight.shape[0]
    head_size = width_here // heads_here
    tile_count = clip_tokens.shape[1] // TILE
    projected = jnp.einsum(
        "ctd,sdh->scth",
        lax.all_gather(clip_tokens, "dp", axis=0, tiled=True),
        qkv_weight,
        preferred_element_type=jnp.float32,
    ).astype(jnp.bfloat16)
    clip_count = projected.shape[1]
    queries = projected[0].reshape(clip_count, tile_count, TILE, heads_here, head_size)
    key_values = projected[1:3].reshape(2, clip_count, tile_count, TILE, width_here)
    own_index = lax.axis_index("ctx")
    offsets = list(range(1, REACH + 1)) + [-amount for amount in range(1, REACH + 1)]
    live_slots = jnp.arange(KMAX)[None, :] < counts[:, None]
    collected = [key_values]
    for offset in offsets:
        collected.append(shifted(key_values, "ctx", offset))
    buffer_tiles = jnp.concatenate(collected, axis=2)
    distance = own_index - neighbours // tile_count
    which_block = jnp.where(distance > 0, distance, jnp.where(distance < 0, REACH - distance, 0))
    position = which_block * tile_count + neighbours % tile_count
    gathered = jnp.take(buffer_tiles, position.reshape(-1), axis=2)
    gathered = gathered.reshape(2, clip_count, tile_count, KMAX, TILE, heads_here, head_size)
    scores = jnp.einsum(
        "ctihd,ctmjhd->cthimj", queries, gathered[0], preferred_element_type=jnp.float32
    ) * (1.0 / math.sqrt(head_size))
    one_hot = (bias_index[:, :, None] == jnp.arange(rel_bias.shape[1])[None, None, :]).astype(
        jnp.float32
    )
    looked_up = jnp.einsum("tmr,hr->thm", one_hot, rel_bias, precision=lax.Precision.HIGHEST)
    scores = scores + looked_up[None, :, :, None, :, None]
    scores = jnp.where(live_slots[None, :, None, None, :, None], scores, -1e30)
    row_max = jnp.max(scores, axis=(4, 5), keepdims=True)
    weights = jnp.exp(scores - row_max)
    weight_sum = jnp.sum(weights, axis=(4, 5))
    blended = jnp.einsum(
        "cthimj,ctmjhd->ctihd",
        weights.astype(jnp.bfloat16),
        gathered[1],
        preferred_element_type=jnp.float32,
    )
    attended = (blended / jnp.transpose(weight_sum, (0, 1, 3, 2))[..., None]).astype(jnp.bfloat16)
    attended = attended.reshape(clip_count, tile_count * TILE, width_here)
    partial_out = jnp.einsum(
        "cth,hd->ctd", attended, out_weight, preferred_element_type=jnp.float32
    ).astype(jnp.bfloat16)
    return lax.psum_scatter(
        lax.optimization_barrier(partial_out).astype(jnp.float32).astype(jnp.bfloat16),
        "dp",
        scatter_dimension=0,
        tiled=True,
    )


def solution(mesh):
    placed = (
        P("dp", "ctx", None),
        P(None, None, "dp"),
        P("dp", None),
        P("ctx", None),
        P("ctx"),
        P("ctx", None),
        P("dp", None),
    )
    return jax.shard_map(
        local, mesh=mesh, in_specs=placed, out_specs=P("dp", "ctx", None), check_vma=False
    )
```

profile of v0, /device:TPU:0, one launch (start us, length us, event | category | flops | bytes accessed | tf_op | source)
XLA Modules:
  0.0 739.2 jit_solution(10897213490841283450)
XLA Ops:
  7.3 74.8 %all-gather.2.cloned.1.call-done = bf16[4,256,3072]{2,1,0:T(8,128)(2,1)} async-done(((bf16[1,256,3072]{2,1,0:T(8,128)(2,1)}), bf16[4,256,3072]{2,1,0:T(8,128)(2,1)}) %all-gather.2.cloned.1.call-update) | async-done | bytes 6291472 | tf_op jit(solution)/shard_map/all_gather | solution.py:25
  82.1 12.5 %convert_bitcast_fusion = bf16[3,4,256,384]{3,2,1,0:T(8,128)(2,1)S(1)} fusion(bf16[4,256,3072]{2,1,0:T(8,128)(2,1)} %all-gather.2.cloned.1.call-done, bf16[3,3072,384]{2,1,0:T(8,128)(2,1)} %param.8), kind=kOutput, calls=%fused_computation.19 | convolution fusion | flops 7248936960 | bytes 15728640 | tf_op jit(solution)/shard_map/ctd,sdh->scth/dot_general | solution.py:23
  100.2 3.6 collective-permute-start.1
  103.8 4.3 collective-permute-start.2
  113.0 27.0 %collective-permute-start.5 = (bf16[2,4,4,64,384]{4,3,2,1,0:T(8,128)(2,1)}, bf16[2,4,4,64,384]{4,3,2,1,0:T(8,128)(2,1)}, u32[]{:S(2)}, u32[]{:S(2)}) collective-permute-start(bf16[2,4,4,64,384]{4,3,2,1,0:T(8,128)(2,1)} %bitcast.4), channel_id=1, source_target_pairs={{0,6},{1,7},{8,14},{9,15},{16,22},{17,23},{24,30},{25,31}} | collective-permute-start | bytes 4718600 | tf_op jit(solution)/shard_map/ppermute | solution.py:15
  141.9 29.6 %collective-permute-done.2 = bf16[2,4,4,64,384]{4,3,2,1,0:T(8,128)(2,1)} collective-permute-done((bf16[2,4,4,64,384]{4,3,2,1,0:T(8,128)(2,1)}, bf16[2,4,4,64,384]{4,3,2,1,0:T(8,128)(2,1)}, u32[]{:S(2)}, u32[]{:S(2)}) %collective-permute-start.2) | collective-permute-done | bytes 1572896 | tf_op jit(solution)/shard_map/ppermute | solution.py:15
  172.8 32.5 %collective-permute-done.3 = bf16[2,4,4,64,384]{4,3,2,1,0:T(8,128)(2,1)} collective-permute-done((bf16[2,4,4,64,384]{4,3,2,1,0:T(8,128)(2,1)}, bf16[2,4,4,64,384]{4,3,2,1,0:T(8,128)(2,1)}, u32[]{:S(2)}, u32[]{:S(2)}) %collective-permute-start.3) | collective-permute-done | bytes 1572896 | tf_op jit(solution)/shard_map/ppermute | solution.py:15
  206.6 32.3 %collective-permute-done.4 = bf16[2,4,4,64,384]{4,3,2,1,0:T(8,128)(2,1)} collective-permute-done((bf16[2,4,4,64,384]{4,3,2,1,0:T(8,128)(2,1)}, bf16[2,4,4,64,384]{4,3,2,1,0:T(8,128)(2,1)}, u32[]{:S(2)}, u32[]{:S(2)}) %collective-permute-start.4) | collective-permute-done | bytes 1572896 | tf_op jit(solution)/shard_map/ppermute | solution.py:15
  240.2 32.4 %collective-permute-done.5 = bf16[2,4,4,64,384]{4,3,2,1,0:T(8,128)(2,1)} collective-permute-done((bf16[2,4,4,64,384]{4,3,2,1,0:T(8,128)(2,1)}, bf16[2,4,4,64,384]{4,3,2,1,0:T(8,128)(2,1)}, u32[]{:S(2)}, u32[]{:S(2)}) %collective-permute-start.5) | collective-permute-done | bytes 1572896 | tf_op jit(solution)/shard_map/ppermute | solution.py:15
  302.0 9.5 %collective-permute-done.7 = bf16[2,4,4,64,384]{4,3,2,1,0:T(8,128)(2,1)} collective-permute-done((bf16[2,4,4,64,384]{4,3,2,1,0:T(8,128)(2,1)}, bf16[2,4,4,64,384]{4,3,2,1,0:T(8,128)(2,1)}, u32[]{:S(2)}, u32[]{:S(2)}) %collective-permute-start.7) | collective-permute-done | bytes 1572896 | tf_op jit(solution)/shard_map/ppermute | solution.py:15
  314.3 66.1 %collective-permute-done.8 = bf16[2,4,4,64,384]{4,3,2,1,0:T(8,128)(2,1)} collective-permute-done((bf16[2,4,4,64,384]{4,3,2,1,0:T(8,128)(2,1)}, bf16[2,4,4,64,384]{4,3,2,1,0:T(8,128)(2,1)}, u32[]{:S(2)}, u32[]{:S(2)}) %collective-permute-start.8) | collective-permute-done | bytes 1572896 | tf_op jit(solution)/shard_map/ppermute | solution.py:15
  385.9 146.2 %collective-permute-done.10 = bf16[2,4,4,64,384]{4,3,2,1,0:T(8,128)(2,1)} collective-permute-done((bf16[2,4,4,64,384]{4,3,2,1,0:T(8,128)(2,1)}, bf16[2,4,4,64,384]{4,3,2,1,0:T(8,128)(2,1)}, u32[]{:S(2)}, u32[]{:S(2)}) %collective-permute-start.10) | collective-permute-done | bytes 1572896 | tf_op jit(solution)/shard_map/ppermute | solution.py:15
  536.2 15.1 %gather_fusion = bf16[40,2,4,64,384]{4,3,2,1,0:T(8,128)(2,1)} fusion(bf16[2,4,52,64,384]{4,3,2,1,0:T(8,128)(2,1)} %constant_dynamic-update-slice_fusion, s32[1024]{0:T(1024)S(1)} %pad_clamp_fusion), kind=kCustom, calls=%fused_computation | custom fusion | bytes 31457440 | tf_op jit(solution)/shard_map/jit(_take)/gather | solution.py:42
  551.3 8.4 %select_bitcast_fusion = bf16[2,4,40,64,384]{4,3,1,0,2:T(8,128)(2,1)S(1)} fusion(bf16[40,2,4,64,384]{4,3,2,1,0:T(8,128)(2,1)} %gather_fusion, pred[40]{0:T(512)(128)(4,1)S(1)} %compare_and_fusion), kind=kLoop, calls=%fused_computation.1 | loop fusion | flops 7864320 | bytes 31457320 | tf_op jit(solution)/shard_map/jit(_take)/select_n | solution.py:42
  559.7 6.3 fusion.35
  566.0 20.6 %reshape.95 = bf16[4,4,10,64,3,128]{5,4,3,0,2,1:T(4,128)(2,1)} reshape(bf16[1,4,40,64,384]{4,3,1,0,2:T(8,128)(2,1)} %get-tuple-element.6) | data formatting | bytes 15728640 | tf_op jit(solution)/shard_map/squeeze | solution.py:45
  586.6 9.4 %copy.25 = bf16[4,4,10,64,3,128]{5,3,2,4,1,0:T(8,128)(2,1)} copy(bf16[4,4,10,64,3,128]{5,4,3,0,2,1:T(4,128)(2,1)} %reshape.95) | data formatting | bytes 15728640 | tf_op jit(solution)/shard_map/squeeze | solution.py:45
  596.0 10.9 %fusion.24 = f32[4,4,3,64,640]{3,4,2,1,0} fusion(bf16[4,4,3,128,640]{3,4,2,1,0:T(8,128)(2,1)} %bitcast.55, bf16[4,4,64,3,128]{4,3,2,1,0:T(4,128)(2,1)S(1)} %reshape_squeeze.3), kind=kOutput, calls=%fused_computation.23 | convolution fusion | flops 503316480 | bytes 16515072
  606.9 8.9 %fusion.2 = f32[4,4,3,64]{3,2,1,0:T(4,128)S(1)} fusion(f32[4,4,3,64,10,64]{3,5,4,2,1,0:T(8,128)} %bitcast.52, f32[4,3,10]{2,1,0:T(4,128)S(1)} %convolution_bitcast_fusion, pred[4,10]{1,0:T(4,128)(4,1)S(1)} %iota_compare_fusion.2), kind=kLoop, calls=%fused_computation.6 | loop fusion | flops 7861248 | bytes 7877128 | tf_op jit(solution)/shard_map/reduce_max | solution.py:53
  615.8 8.0 %fusion = f32[4,4,3,64]{3,2,1,0:T(4,128)S(1)} fusion(f32[4,4,3,64,10,64]{3,5,4,2,1,0:T(8,128)} %bitcast.53, f32[4,4,3,64]{3,2,1,0:T(4,128)S(1)} %fusion.2, f32[4,3,10]{2,1,0:T(4,128)S(1)} %convolution_bitcast_fusion, pred[4,10]{1,0:T(4,128)(4,1)S(1)} %iota_compare_fusion.2), kind=kLoop, calls=%fused_computation.4 | loop fusion | flops 9827328 | bytes 7889416 | tf_op jit(solution)/shard_map/reduce_sum | solution.py:55
  623.8 20.7 %reshape.94 = bf16[4,4,10,64,3,128]{5,4,3,0,2,1:T(4,128)(2,1)} reshape(bf16[1,4,40,64,384]{4,3,1,0,2:T(8,128)(2,1)} %get-tuple-element.5) | data formatting | bytes 15728640 | tf_op jit(solution)/shard_map/squeeze | solution.py:59
  644.5 11.6 %fusion.19 = bf16[4,4,64,3,128]{4,2,3,1,0:T(8,128)(2,1)S(1)} fusion(f32[4,4,3,64,10,64]{3,5,4,2,1,0:T(8,128)} %bitcast.54, f32[4,4,3,64]{3,2,1,0:T(4,128)S(1)} %fusion.2, f32[4,3,10]{2,1,0:T(4,128)S(1)} %convolution_bitcast_fusion, pred[4,10]{1,0:T(4,128)(4,1)S(1)} %iota_compare_fusion.2, bf16[4,4,10,64,3,128]{5,4,3,0,2,1:T(4,128)(2,1)} %reshape.94, ...), kind=kOutput, calls=%fused_computation.21 | convolution fusion | flops 513933312 | bytes 16540168 | tf_op jit(solution)/shard_map/cthimj,ctmjhd->ctihd/dot_general | solution.py:56
  658.2 6.5 convolution_convert_fusion
  664.7 67.6 %reduce-scatter.4.cloned.1.call-done = bf16[1,256,3072]{2,1,0:T(8,128)(2,1)} async-done(((bf16[4,256,3072]{2,1,0:T(8,128)(2,1)}), bf16[1,256,3072]{2,1,0:T(8,128)(2,1)}) %reduce-scatter.4.cloned.1.call-update) | async-done | bytes 1572880
  (56 shorter events, 60.9 us)
Async XLA Ops:
  6.5 651.7 %copy-start = (bf16[384,3072]{1,0:T(8,128)(2,1)S(1)}, bf16[384,3072]{1,0:T(8,128)(2,1)}, u32[]{:S(2)}) copy-start(bf16[384,3072]{1,0:T(8,128)(2,1)} %param.9) | copy-start | bytes 7077892
  6.5 75.6 %all-gather.2.cloned.1.call-start = ((), (), s32[]{:S(2)}) async-start(), calls=%async_computation.1 | async-start | bytes 7864320 | tf_op jit(solution)/shard_map/all_gather | solution.py:25
  7.3 134.0 %copy-start.2 = (s32[4,10]{1,0:T(4,128)S(1)}, s32[4,10]{1,0:T(4,128)}, u32[]{:S(2)}) copy-start(s32[4,10]{1,0:T(4,128)} %param.10) | copy-start | bytes 484
  7.3 134.2 %copy-start.3 = (f32[3,343]{1,0:T(4,128)S(1)}, f32[3,343]{1,0:T(4,128)}, u32[]{:S(2)}) copy-start(f32[3,343]{1,0:T(4,128)} %param.13) | copy-start | bytes 12352
  7.3 134.2 %copy-start.4 = (s32[4,10]{1,0:T(4,128)S(1)}, s32[4,10]{1,0:T(4,128)}, u32[]{:S(2)}) copy-start(s32[4,10]{1,0:T(4,128)} %param.12) | copy-start | bytes 484
  7.3 199.2 %copy-start.5 = (s32[4]{0:T(128)S(1)}, s32[4]{0:T(128)}, u32[]{:S(2)}) copy-start(s32[4]{0:T(128)} %param.11) | copy-start | bytes 52
  7.3 725.0 %reduce-scatter.4.cloned.1.call-start = ((), (), s32[]{:S(2)}) async-start(), calls=%async_computation.2 | async-start | bytes 7864320
  94.6 1.4 copy-start.1
  97.3 15.7 %collective-permute-start = (bf16[2,4,4,64,384]{4,3,2,1,0:T(8,128)(2,1)}, bf16[2,4,4,64,384]{4,3,2,1,0:T(8,128)(2,1)}, u32[]{:S(2)}, u32[]{:S(2)}) collective-permute-start(bf16[2,4,4,64,384]{4,3,2,1,0:T(8,128)(2,1)} %bitcast.4), channel_id=1, source_target_pairs={{0,1},{1,2},{2,3},{3,4},{4,5},{5,6},{6,7},{8,9},{9,10},{10,11},{11... | collective-permute-start | bytes 4718600 | tf_op jit(solution)/shard_map/ppermute | solution.py:15
  100.2 39.8 %collective-permute-start.1 = (bf16[2,4,4,64,384]{4,3,2,1,0:T(8,128)(2,1)}, bf16[2,4,4,64,384]{4,3,2,1,0:T(8,128)(2,1)}, u32[]{:S(2)}, u32[]{:S(2)}) collective-permute-start(bf16[2,4,4,64,384]{4,3,2,1,0:T(8,128)(2,1)} %bitcast.4), channel_id=1, source_target_pairs={{0,2},{1,3},{2,4},{3,5},{4,6},{5,7},{8,10},{9,11},{10,12},{11,13},... | collective-permute-start | bytes 4718600 | tf_op jit(solution)/shard_map/ppermute | solution.py:15
  103.8 67.7 %collective-permute-start.2 = (bf16[2,4,4,64,384]{4,3,2,1,0:T(8,128)(2,1)}, bf16[2,4,4,64,384]{4,3,2,1,0:T(8,128)(2,1)}, u32[]{:S(2)}, u32[]{:S(2)}) collective-permute-start(bf16[2,4,4,64,384]{4,3,2,1,0:T(8,128)(2,1)} %bitcast.4), channel_id=1, source_target_pairs={{0,3},{1,4},{2,5},{3,6},{4,7},{8,11},{9,12},{10,13},{11,14},{12,15... | collective-permute-start | bytes 4718600 | tf_op jit(solution)/shard_map/ppermute | solution.py:15
  108.1 97.2 %collective-permute-start.3 = (bf16[2,4,4,64,384]{4,3,2,1,0:T(8,128)(2,1)}, bf16[2,4,4,64,384]{4,3,2,1,0:T(8,128)(2,1)}, u32[]{:S(2)}, u32[]{:S(2)}) collective-permute-start(bf16[2,4,4,64,384]{4,3,2,1,0:T(8,128)(2,1)} %bitcast.4), channel_id=1, source_target_pairs={{0,4},{1,5},{2,6},{3,7},{8,12},{9,13},{10,14},{11,15},{16,20},{17,... | collective-permute-start | bytes 4718600 | tf_op jit(solution)/shard_map/ppermute | solution.py:15
  110.5 128.4 %collective-permute-start.4 = (bf16[2,4,4,64,384]{4,3,2,1,0:T(8,128)(2,1)}, bf16[2,4,4,64,384]{4,3,2,1,0:T(8,128)(2,1)}, u32[]{:S(2)}, u32[]{:S(2)}) collective-permute-start(bf16[2,4,4,64,384]{4,3,2,1,0:T(8,128)(2,1)} %bitcast.4), channel_id=1, source_target_pairs={{0,5},{1,6},{2,7},{8,13},{9,14},{10,15},{16,21},{17,22},{18,23},{2... | collective-permute-start | bytes 4718600 | tf_op jit(solution)/shard_map/ppermute | solution.py:15
  113.0 159.7 %collective-permute-start.5 = (bf16[2,4,4,64,384]{4,3,2,1,0:T(8,128)(2,1)}, bf16[2,4,4,64,384]{4,3,2,1,0:T(8,128)(2,1)}, u32[]{:S(2)}, u32[]{:S(2)}) collective-permute-start(bf16[2,4,4,64,384]{4,3,2,1,0:T(8,128)(2,1)} %bitcast.4), channel_id=1, source_target_pairs={{0,6},{1,7},{8,14},{9,15},{16,22},{17,23},{24,30},{25,31}} | collective-permute-start | bytes 4718600 | tf_op jit(solution)/shard_map/ppermute | solution.py:15
  140.0 141.2 %collective-permute-start.6 = (bf16[2,4,4,64,384]{4,3,2,1,0:T(8,128)(2,1)}, bf16[2,4,4,64,384]{4,3,2,1,0:T(8,128)(2,1)}, u32[]{:S(2)}, u32[]{:S(2)}) collective-permute-start(bf16[2,4,4,64,384]{4,3,2,1,0:T(8,128)(2,1)} %bitcast.4), channel_id=1, source_target_pairs={{1,0},{2,1},{3,2},{4,3},{5,4},{6,5},{7,6},{9,8},{10,9},{11,10},{12... | collective-permute-start | bytes 4718600 | tf_op jit(solution)/shard_map/ppermute | solution.py:15
  171.5 140.1 %collective-permute-start.7 = (bf16[2,4,4,64,384]{4,3,2,1,0:T(8,128)(2,1)}, bf16[2,4,4,64,384]{4,3,2,1,0:T(8,128)(2,1)}, u32[]{:S(2)}, u32[]{:S(2)}) collective-permute-start(bf16[2,4,4,64,384]{4,3,2,1,0:T(8,128)(2,1)} %bitcast.4), channel_id=1, source_target_pairs={{2,0},{3,1},{4,2},{5,3},{6,4},{7,5},{10,8},{11,9},{12,10},{13,11},... | collective-permute-start | bytes 4718600 | tf_op jit(solution)/shard_map/ppermute | solution.py:15
  205.2 175.2 %collective-permute-start.8 = (bf16[2,4,4,64,384]{4,3,2,1,0:T(8,128)(2,1)}, bf16[2,4,4,64,384]{4,3,2,1,0:T(8,128)(2,1)}, u32[]{:S(2)}, u32[]{:S(2)}) collective-permute-start(bf16[2,4,4,64,384]{4,3,2,1,0:T(8,128)(2,1)} %bitcast.4), channel_id=1, source_target_pairs={{3,0},{4,1},{5,2},{6,3},{7,4},{11,8},{12,9},{13,10},{14,11},{15,12... | collective-permute-start | bytes 4718600 | tf_op jit(solution)/shard_map/ppermute | solution.py:15
  238.9 144.2 %collective-permute-start.9 = (bf16[2,4,4,64,384]{4,3,2,1,0:T(8,128)(2,1)}, bf16[2,4,4,64,384]{4,3,2,1,0:T(8,128)(2,1)}, u32[]{:S(2)}, u32[]{:S(2)}) collective-permute-start(bf16[2,4,4,64,384]{4,3,2,1,0:T(8,128)(2,1)} %bitcast.4), channel_id=1, source_target_pairs={{4,0},{5,1},{6,2},{7,3},{12,8},{13,9},{14,10},{15,11},{20,16},{21,... | collective-permute-start | bytes 4718600 | tf_op jit(solution)/shard_map/ppermute | solution.py:15
  272.6 259.4 %collective-permute-start.10 = (bf16[2,4,4,64,384]{4,3,2,1,0:T(8,128)(2,1)}, bf16[2,4,4,64,384]{4,3,2,1,0:T(8,128)(2,1)}, u32[]{:S(2)}, u32[]{:S(2)}) collective-permute-start(bf16[2,4,4,64,384]{4,3,2,1,0:T(8,128)(2,1)} %bitcast.4), channel_id=1, source_target_pairs={{5,0},{6,1},{7,2},{13,8},{14,9},{15,10},{21,16},{22,17},{23,18},{2... | collective-permute-start | bytes 4718600 | tf_op jit(solution)/shard_map/ppermute | solution.py:15
  281.2 253.6 %collective-permute-start.11 = (bf16[2,4,4,64,384]{4,3,2,1,0:T(8,128)(2,1)}, bf16[2,4,4,64,384]{4,3,2,1,0:T(8,128)(2,1)S(1)}, u32[]{:S(2)}, u32[]{:S(2)}) collective-permute-start(bf16[2,4,4,64,384]{4,3,2,1,0:T(8,128)(2,1)} %bitcast.4), channel_id=1, source_target_pairs={{6,0},{7,1},{14,8},{15,9},{22,16},{23,17},{30,24},{31,25}} | collective-permute-start | bytes 4718600 | tf_op jit(solution)/shard_map/ppermute | solution.py:15
Sparse Core Ops, SparseCore 0:
  9.2 72.8 all-gather.1
  664.9 67.4 reduce-scatter.3
where the time goes:
time: 741 us; the launch traced here: 739 us
  waiting for transfers between devices  492 us (66%)
  local copies, waits for them, and re-layouts  116 us (16%)
  starting transfers between devices  50.4 us (7%)
  matrix products  41.9 us (6%)
  other arithmetic  25.4 us (3%)
  between operations  13.6 us (2%)
    ppermute x12, waiting for transfers between devices, shifted(): lax.ppermute(value, axis, [(source, source + steps) for source in range(f...  349 us
    all_gather x1, waiting for transfers between devices, local(): lax.all_gather(clip_tokens, 'dp', axis=0, tiled=True)  74.8 us
    unnamed x3, waiting for transfers between devices  68.3 us
    ppermute x12, starting transfers between devices, shifted(): lax.ppermute(value, axis, [(source, source + steps) for source in range(f...  50.4 us
    unnamed x24, local copies, waits for them, and re-layouts  34.7 us
    squeeze x2, local copies, waits for them, and re-layouts, local(): gathered[0]  30 us
    squeeze x1, local copies, waits for them, and re-layouts, local(): gathered[1]  20.7 us
    gather x1, local copies, waits for them, and re-layouts, local(): gathered = jnp.take(buffer_tiles, position.reshape(-1), axis=2)  15.1 us
  transfers between devices with their start and end apart: 14, of which 9 were waited for; matrix products, arithmetic and copies ran while one was open for 5% of the time, Pallas kernels for 0%

commit v1 on v0

--- a/solution.py
+++ b/solution.py
@@ -9,6 +9,12 @@
 KMAX = 10
 
 
+def _spread_point(xx, which_dim):
+    xx = jnp.moveaxis(xx, 0, which_dim)
+    now = xx.shape
+    return xx.reshape(*now[:which_dim], now[which_dim] * now[which_dim + 1], *now[which_dim + 2 :])
+
+
 def shifted(value, axis, steps):
     count = lax.axis_size(axis)
     first, last = (max(0, -steps), min(count, count - steps))
@@ -16,13 +22,34 @@
 
 
 def local(clip_tokens, qkv_weight, out_weight, neighbours, counts, bias_index, rel_bias):
+
+    def group_area_on_mesh(x_in, bus_axis, in_dim=0):
+        slots = lax.axis_size(bus_axis)
+        column = [(j, (j + 1) % slots) for j in range(slots)]
+        tray = [(h, kk) for kk, h in column]
+        res, then = ([], [])
+        src_i = 0
+        while src_i < slots - 1:
+            if src_i % 2 == 0:
+                big = lax.ppermute(res[-1] if res else x_in, bus_axis, perm=column)
+                res.append(big)
+            else:
+                latest = lax.ppermute(then[-1] if then else x_in, bus_axis, tray)
+                then.append(latest)
+            src_i += 1
+        a_now = jnp.stack([*res[::-1], x_in, *then], axis=0)
+        passed = lax.axis_index(bus_axis)
+        main = passed - len(res)
+        a_now = a_now[(jnp.arange(slots) - main) % slots]
+        return _spread_point(a_now, in_dim)
+
     heads_here = rel_bias.shape[0]
     width_here = out_weight.shape[0]
     head_size = width_here // heads_here
     tile_count = clip_tokens.shape[1] // TILE
     projected = jnp.einsum(
         "ctd,sdh->scth",
-        lax.all_gather(clip_tokens, "dp", axis=0, tiled=True),
+        group_area_on_mesh(clip_tokens, "dp"),
         qkv_weight,
         preferred_element_type=jnp.float32,
     ).astype(jnp.bfloat16)

time: 741 us -> 785 us (1.059)
  waiting for transfers between devices: 492 us -> 520 us
    ppermute x0 -> x3, waiting for transfers between devices: none -> 101 us  [the longest x2 67.8 us: group_area_on_mesh(): big = lax.ppermute(res[-1] if res else x_in, bus_axis, perm=column)]
    all_gather x1 -> x0, waiting for transfers between devices: 74.8 us -> none  [local(): lax.all_gather(clip_tokens, 'dp', axis=0, tiled=True)]
    unnamed x24 -> x23, local copies, waits for them, and re-layouts: 34.7 us -> 30.4 us
    unnamed x3 -> x2, waiting for transfers between devices: 68.3 us -> 67.7 us
  transfers between devices with their start and end apart: 14 -> 16, of which waited for: 9 -> 11; matrix products, arithmetic and copies ran while one was open for 5% -> 5% of each run, Pallas kernels for 0% -> 0%
where the time goes in v1:
time: 785 us; the launch traced here: 783 us
  waiting for transfers between devices  520 us (66%)
  local copies, waits for them, and re-layouts  119 us (15%)
  starting transfers between devices  55.9 us (7%)
  matrix products  41.8 us (5%)
  other arithmetic  32 us (4%)
  between operations  13.6 us (2%)
    ppermute x12, waiting for transfers between devices, shifted(): lax.ppermute(value, axis, [(source, source + steps) for source in range(f...  351 us
    ppermute x2, waiting for transfers between devices, group_area_on_mesh(): big = lax.ppermute(res[-1] if res else x_in, bus_axis, perm=column)  67.8 us
    unnamed x2, waiting for transfers between devices  67.7 us
    ppermute x12, starting transfers between devices, shifted(): lax.ppermute(value, axis, [(source, source + steps) for source in range(f...  50.9 us
    ppermute x1, waiting for transfers between devices, group_area_on_mesh(): latest = lax.ppermute(then[-1] if then else x_in, bus_axis, tray)  33.1 us
    unnamed x23, local copies, waits for them, and re-layouts  30.4 us
    squeeze x2, local copies, waits for them, and re-layouts, local(): gathered[0]  30 us
    squeeze x1, local copies, waits for them, and re-layouts, local(): gathered[1]  20.6 us
  transfers between devices with their start and end apart: 16, of which 11 were waited for; matrix products, arithmetic and copies ran while one was open for 5% of the time, Pallas kernels for 0%

profile of v1, /device:TPU:0, one launch (start us, length us, event | category | flops | bytes accessed | tf_op | source)
XLA Modules:
  0.0 782.6 jit_solution(6514735494726844025)
XLA Ops:
  10.4 35.5 %collective-permute-done = bf16[1,256,3072]{2,1,0:T(8,128)(2,1)} collective-permute-done((bf16[1,256,3072]{2,1,0:T(8,128)(2,1)}, bf16[1,256,3072]{2,1,0:T(8,128)(2,1)}, u32[]{:S(2)}, u32[]{:S(2)}) %collective-permute-start) | collective-permute-done | bytes 1572896 | tf_op jit(solution)/shard_map/ppermute | solution.py:34
  47.1 33.1 %collective-permute-done.2 = bf16[1,256,3072]{2,1,0:T(8,128)(2,1)} collective-permute-done((bf16[1,256,3072]{2,1,0:T(8,128)(2,1)}, bf16[1,256,3072]{2,1,0:T(8,128)(2,1)}, u32[]{:S(2)}, u32[]{:S(2)}) %collective-permute-start.2) | collective-permute-done | bytes 1572896 | tf_op jit(solution)/shard_map/ppermute | solution.py:37
  80.2 32.3 %collective-permute-done.1 = bf16[1,256,3072]{2,1,0:T(8,128)(2,1)} collective-permute-done((bf16[1,256,3072]{2,1,0:T(8,128)(2,1)}, bf16[1,256,3072]{2,1,0:T(8,128)(2,1)}, u32[]{:S(2)}, u32[]{:S(2)}) %collective-permute-start.1) | collective-permute-done | bytes 1572896 | tf_op jit(solution)/shard_map/ppermute | solution.py:34
  112.6 6.5 maximum_bitcast_fusion
  125.5 12.4 %convert_bitcast_fusion = bf16[3,4,256,384]{3,2,0,1:T(8,128)(2,1)S(1)} fusion(bf16[3,3072,384]{2,1,0:T(8,128)(2,1)} %param.8, bf16[4,256,3072]{2,1,0:T(8,128)(2,1)} %gather_fusion), kind=kOutput, calls=%fused_computation.21 | convolution fusion | flops 7248936960 | bytes 15728640 | tf_op jit(solution)/shard_map/ctd,sdh->scth/dot_general | solution.py:50
  156.5 27.0 %collective-permute-start.8 = (bf16[2,4,4,64,384]{4,3,2,1,0:T(8,128)(2,1)}, bf16[2,4,4,64,384]{4,3,2,1,0:T(8,128)(2,1)}, u32[]{:S(2)}, u32[]{:S(2)}) collective-permute-start(bf16[2,4,4,64,384]{4,3,2,1,0:T(8,128)(2,1)} %get-tuple-element.7), channel_id=1, source_target_pairs={{0,6},{1,7},{8,14},{9,15},{16,22},{17,23},{24,30},{25,31}} | collective-permute-start | bytes 4718600 | tf_op jit(solution)/shard_map/ppermute | solution.py:21
  185.5 29.4 %collective-permute-done.5 = bf16[2,4,4,64,384]{4,3,2,1,0:T(8,128)(2,1)} collective-permute-done((bf16[2,4,4,64,384]{4,3,2,1,0:T(8,128)(2,1)}, bf16[2,4,4,64,384]{4,3,2,1,0:T(8,128)(2,1)}, u32[]{:S(2)}, u32[]{:S(2)}) %collective-permute-start.5) | collective-permute-done | bytes 1572896 | tf_op jit(solution)/shard_map/ppermute | solution.py:21
  216.1 32.5 %collective-permute-done.6 = bf16[2,4,4,64,384]{4,3,2,1,0:T(8,128)(2,1)} collective-permute-done((bf16[2,4,4,64,384]{4,3,2,1,0:T(8,128)(2,1)}, bf16[2,4,4,64,384]{4,3,2,1,0:T(8,128)(2,1)}, u32[]{:S(2)}, u32[]{:S(2)}) %collective-permute-start.6) | collective-permute-done | bytes 1572896 | tf_op jit(solution)/shard_map/ppermute | solution.py:21
  249.9 32.4 %collective-permute-done.7 = bf16[2,4,4,64,384]{4,3,2,1,0:T(8,128)(2,1)} collective-permute-done((bf16[2,4,4,64,384]{4,3,2,1,0:T(8,128)(2,1)}, bf16[2,4,4,64,384]{4,3,2,1,0:T(8,128)(2,1)}, u32[]{:S(2)}, u32[]{:S(2)}) %collective-permute-start.7) | collective-permute-done | bytes 1572896 | tf_op jit(solution)/shard_map/ppermute | solution.py:21
  283.7 32.3 %collective-permute-done.8 = bf16[2,4,4,64,384]{4,3,2,1,0:T(8,128)(2,1)} collective-permute-done((bf16[2,4,4,64,384]{4,3,2,1,0:T(8,128)(2,1)}, bf16[2,4,4,64,384]{4,3,2,1,0:T(8,128)(2,1)}, u32[]{:S(2)}, u32[]{:S(2)}) %collective-permute-start.8) | collective-permute-done | bytes 1572896 | tf_op jit(solution)/shard_map/ppermute | solution.py:21
  342.5 12.5 %collective-permute-done.10 = bf16[2,4,4,64,384]{4,3,2,1,0:T(8,128)(2,1)} collective-permute-done((bf16[2,4,4,64,384]{4,3,2,1,0:T(8,128)(2,1)}, bf16[2,4,4,64,384]{4,3,2,1,0:T(8,128)(2,1)}, u32[]{:S(2)}, u32[]{:S(2)}) %collective-permute-start.10) | collective-permute-done | bytes 1572896 | tf_op jit(solution)/shard_map/ppermute | solution.py:21
  357.7 66.1 %collective-permute-done.11 = bf16[2,4,4,64,384]{4,3,2,1,0:T(8,128)(2,1)} collective-permute-done((bf16[2,4,4,64,384]{4,3,2,1,0:T(8,128)(2,1)}, bf16[2,4,4,64,384]{4,3,2,1,0:T(8,128)(2,1)}, u32[]{:S(2)}, u32[]{:S(2)}) %collective-permute-start.11) | collective-permute-done | bytes 1572896 | tf_op jit(solution)/shard_map/ppermute | solution.py:21
  429.3 146.2 %collective-permute-done.13 = bf16[2,4,4,64,384]{4,3,2,1,0:T(8,128)(2,1)} collective-permute-done((bf16[2,4,4,64,384]{4,3,2,1,0:T(8,128)(2,1)}, bf16[2,4,4,64,384]{4,3,2,1,0:T(8,128)(2,1)}, u32[]{:S(2)}, u32[]{:S(2)}) %collective-permute-start.13) | collective-permute-done | bytes 1572896 | tf_op jit(solution)/shard_map/ppermute | solution.py:21
  579.6 15.1 %gather_fusion.1 = bf16[40,2,4,64,384]{4,3,2,1,0:T(8,128)(2,1)} fusion(bf16[2,4,52,64,384]{4,3,2,1,0:T(8,128)(2,1)} %constant_dynamic-update-slice_fusion, s32[1024]{0:T(1024)S(1)} %pad_clamp_fusion), kind=kCustom, calls=%fused_computation.1 | custom fusion | bytes 31457440 | tf_op jit(solution)/shard_map/jit(_take)/gather | solution.py:69
  594.7 8.4 %select_bitcast_fusion = bf16[2,4,40,64,384]{4,3,1,0,2:T(8,128)(2,1)S(1)} fusion(bf16[40,2,4,64,384]{4,3,2,1,0:T(8,128)(2,1)} %gather_fusion.1, pred[40]{0:T(512)(128)(4,1)S(1)} %compare_and_fusion), kind=kLoop, calls=%fused_computation.2 | loop fusion | flops 7864320 | bytes 31457320 | tf_op jit(solution)/shard_map/jit(_take)/select_n | solution.py:69
  609.4 20.6 %reshape.159 = bf16[4,4,10,64,3,128]{5,4,3,0,2,1:T(4,128)(2,1)} reshape(bf16[1,4,40,64,384]{4,3,1,0,2:T(8,128)(2,1)} %get-tuple-element.6) | data formatting | bytes 15728640 | tf_op jit(solution)/shard_map/squeeze | solution.py:72
  630.0 9.4 %copy.51 = bf16[4,4,10,64,3,128]{5,3,2,4,1,0:T(8,128)(2,1)} copy(bf16[4,4,10,64,3,128]{5,4,3,0,2,1:T(4,128)(2,1)} %reshape.159) | data formatting | bytes 15728640 | tf_op jit(solution)/shard_map/squeeze | solution.py:72
  639.4 10.9 %fusion.24 = f32[4,4,3,64,640]{3,4,2,1,0} fusion(bf16[4,4,3,128,640]{3,4,2,1,0:T(8,128)(2,1)} %bitcast.65, bf16[4,4,64,3,128]{4,3,2,1,0:T(4,128)(2,1)S(1)} %reshape_squeeze.3), kind=kOutput, calls=%fused_computation.25 | convolution fusion | flops 503316480 | bytes 16515072
  650.4 8.9 %fusion.2 = f32[4,4,3,64]{3,2,1,0:T(4,128)S(1)} fusion(f32[4,4,3,64,10,64]{3,5,4,2,1,0:T(8,128)} %bitcast.62, f32[4,3,10]{2,1,0:T(4,128)S(1)} %convolution_bitcast_fusion, pred[4,10]{1,0:T(4,128)(4,1)S(1)} %iota_compare_fusion.2), kind=kLoop, calls=%fused_computation.7 | loop fusion | flops 7861248 | bytes 7877128 | tf_op jit(solution)/shard_map/reduce_max | solution.py:80
  659.3 8.0 %fusion = f32[4,4,3,64]{3,2,1,0:T(4,128)S(1)} fusion(f32[4,4,3,64,10,64]{3,5,4,2,1,0:T(8,128)} %bitcast.63, f32[4,4,3,64]{3,2,1,0:T(4,128)S(1)} %fusion.2, f32[4,3,10]{2,1,0:T(4,128)S(1)} %convolution_bitcast_fusion, pred[4,10]{1,0:T(4,128)(4,1)S(1)} %iota_compare_fusion.2), kind=kLoop, calls=%fused_computation.5 | loop fusion | flops 9827328 | bytes 7889416 | tf_op jit(solution)/shard_map/reduce_sum | solution.py:82
  667.3 20.6 %reshape.158 = bf16[4,4,10,64,3,128]{5,4,3,0,2,1:T(4,128)(2,1)} reshape(bf16[1,4,40,64,384]{4,3,1,0,2:T(8,128)(2,1)} %get-tuple-element.5) | data formatting | bytes 15728640 | tf_op jit(solution)/shard_map/squeeze | solution.py:86
  687.9 11.6 %fusion.19 = bf16[4,4,64,3,128]{4,2,3,1,0:T(8,128)(2,1)S(1)} fusion(f32[4,4,3,64,10,64]{3,5,4,2,1,0:T(8,128)} %bitcast.64, f32[4,4,3,64]{3,2,1,0:T(4,128)S(1)} %fusion.2, f32[4,3,10]{2,1,0:T(4,128)S(1)} %convolution_bitcast_fusion, pred[4,10]{1,0:T(4,128)(4,1)S(1)} %iota_compare_fusion.2, bf16[4,4,10,64,3,128]{5,4,3,0,2,1:T(4,128)(2,1)} %reshape.158, ...), kind=kOutput, calls=%fused_computation.23 | convolution fusion | flops 513933312 | bytes 16540168 | tf_op jit(solution)/shard_map/cthimj,ctmjhd->ctihd/dot_general | solution.py:83
  701.6 6.5 convolution_convert_fusion
  708.1 67.7 %reduce-scatter.4.cloned.1.call-done = bf16[1,256,3072]{2,1,0:T(8,128)(2,1)} async-done(((bf16[4,256,3072]{2,1,0:T(8,128)(2,1)}), bf16[1,256,3072]{2,1,0:T(8,128)(2,1)}) %reduce-scatter.4.cloned.1.call-update) | async-done | bytes 1572880
  (63 shorter events, 82.9 us)
Async XLA Ops:
  6.5 695.1 %copy-start = (bf16[384,3072]{1,0:T(8,128)(2,1)S(1)}, bf16[384,3072]{1,0:T(8,128)(2,1)}, u32[]{:S(2)}) copy-start(bf16[384,3072]{1,0:T(8,128)(2,1)} %param.9) | copy-start | bytes 7077892
  6.5 769.2 %reduce-scatter.4.cloned.1.call-start = ((), (), s32[]{:S(2)}) async-start(), calls=%async_computation.1 | async-start | bytes 7864320
  6.5 39.4 %collective-permute-start = (bf16[1,256,3072]{2,1,0:T(8,128)(2,1)}, bf16[1,256,3072]{2,1,0:T(8,128)(2,1)}, u32[]{:S(2)}, u32[]{:S(2)}) collective-permute-start(bf16[1,256,3072]{2,1,0:T(8,128)(2,1)} %param.7), channel_id=1, source_target_pairs={{0,8},{8,16},{16,24},{24,0},{1,9},{9,17},{17,25},{25,1},{2,10},{10... | collective-permute-start | bytes 4718600 | tf_op jit(solution)/shard_map/ppermute | solution.py:34
  9.5 70.8 %collective-permute-start.2 = (bf16[1,256,3072]{2,1,0:T(8,128)(2,1)}, bf16[1,256,3072]{2,1,0:T(8,128)(2,1)}, u32[]{:S(2)}, u32[]{:S(2)}) collective-permute-start(bf16[1,256,3072]{2,1,0:T(8,128)(2,1)} %param.7), channel_id=1, source_target_pairs={{8,0},{16,8},{24,16},{0,24},{9,1},{17,9},{25,17},{1,25},{10,2},{18... | collective-permute-start | bytes 4718600 | tf_op jit(solution)/shard_map/ppermute | solution.py:37
  46.0 66.6 %collective-permute-start.1 = (bf16[1,256,3072]{2,1,0:T(8,128)(2,1)}, bf16[1,256,3072]{2,1,0:T(8,128)(2,1)}, u32[]{:S(2)}, u32[]{:S(2)}) collective-permute-start(bf16[1,256,3072]{2,1,0:T(8,128)(2,1)} %collective-permute-done), channel_id=1, source_target_pairs={{0,8},{8,16},{16,24},{24,0},{1,9},{9,17},{17,25},{25,1},{2,10},{10... | collective-permute-start | bytes 4718600 | tf_op jit(solution)/shard_map/ppermute | solution.py:34
  137.9 2.5 copy-start.1
  137.9 46.9 %copy-start.2 = (s32[4,10]{1,0:T(4,128)S(1)}, s32[4,10]{1,0:T(4,128)}, u32[]{:S(2)}) copy-start(s32[4,10]{1,0:T(4,128)} %param.10) | copy-start | bytes 484
  137.9 47.1 %copy-start.3 = (f32[3,343]{1,0:T(4,128)S(1)}, f32[3,343]{1,0:T(4,128)}, u32[]{:S(2)}) copy-start(f32[3,343]{1,0:T(4,128)} %param.13) | copy-start | bytes 12352
  137.9 47.1 %copy-start.4 = (s32[4,10]{1,0:T(4,128)S(1)}, s32[4,10]{1,0:T(4,128)}, u32[]{:S(2)}) copy-start(s32[4,10]{1,0:T(4,128)} %param.12) | copy-start | bytes 484
  138.0 145.6 %copy-start.5 = (s32[4]{0:T(128)S(1)}, s32[4]{0:T(128)}, u32[]{:S(2)}) copy-start(s32[4]{0:T(128)} %param.11) | copy-start | bytes 52
  140.4 16.1 %collective-permute-start.3 = (bf16[2,4,4,64,384]{4,3,2,1,0:T(8,128)(2,1)}, bf16[2,4,4,64,384]{4,3,2,1,0:T(8,128)(2,1)}, u32[]{:S(2)}, u32[]{:S(2)}) collective-permute-start(bf16[2,4,4,64,384]{4,3,2,1,0:T(8,128)(2,1)} %get-tuple-element.7), channel_id=1, source_target_pairs={{0,1},{1,2},{2,3},{3,4},{4,5},{5,6},{6,7},{8,9},{9,10},{10,11},{11... | collective-permute-start | bytes 4718600 | tf_op jit(solution)/shard_map/ppermute | solution.py:21
  142.8 40.7 %collective-permute-start.4 = (bf16[2,4,4,64,384]{4,3,2,1,0:T(8,128)(2,1)}, bf16[2,4,4,64,384]{4,3,2,1,0:T(8,128)(2,1)}, u32[]{:S(2)}, u32[]{:S(2)}) collective-permute-start(bf16[2,4,4,64,384]{4,3,2,1,0:T(8,128)(2,1)} %get-tuple-element.7), channel_id=1, source_target_pairs={{0,2},{1,3},{2,4},{3,5},{4,6},{5,7},{8,10},{9,11},{10,12},{11,13},... | collective-permute-start | bytes 4718600 | tf_op jit(solution)/shard_map/ppermute | solution.py:21
  147.1 67.7 %collective-permute-start.5 = (bf16[2,4,4,64,384]{4,3,2,1,0:T(8,128)(2,1)}, bf16[2,4,4,64,384]{4,3,2,1,0:T(8,128)(2,1)}, u32[]{:S(2)}, u32[]{:S(2)}) collective-permute-start(bf16[2,4,4,64,384]{4,3,2,1,0:T(8,128)(2,1)} %get-tuple-element.7), channel_id=1, source_target_pairs={{0,3},{1,4},{2,5},{3,6},{4,7},{8,11},{9,12},{10,13},{11,14},{12,15... | collective-permute-start | bytes 4718600 | tf_op jit(solution)/shard_map/ppermute | solution.py:21
  151.6 97.0 %collective-permute-start.6 = (bf16[2,4,4,64,384]{4,3,2,1,0:T(8,128)(2,1)}, bf16[2,4,4,64,384]{4,3,2,1,0:T(8,128)(2,1)}, u32[]{:S(2)}, u32[]{:S(2)}) collective-permute-start(bf16[2,4,4,64,384]{4,3,2,1,0:T(8,128)(2,1)} %get-tuple-element.7), channel_id=1, source_target_pairs={{0,4},{1,5},{2,6},{3,7},{8,12},{9,13},{10,14},{11,15},{16,20},{17,... | collective-permute-start | bytes 4718600 | tf_op jit(solution)/shard_map/ppermute | solution.py:21
  154.1 128.2 %collective-permute-start.7 = (bf16[2,4,4,64,384]{4,3,2,1,0:T(8,128)(2,1)}, bf16[2,4,4,64,384]{4,3,2,1,0:T(8,128)(2,1)}, u32[]{:S(2)}, u32[]{:S(2)}) collective-permute-start(bf16[2,4,4,64,384]{4,3,2,1,0:T(8,128)(2,1)} %get-tuple-element.7), channel_id=1, source_target_pairs={{0,5},{1,6},{2,7},{8,13},{9,14},{10,15},{16,21},{17,22},{18,23},{2... | collective-permute-start | bytes 4718600 | tf_op jit(solution)/shard_map/ppermute | solution.py:21
  156.5 159.5 %collective-permute-start.8 = (bf16[2,4,4,64,384]{4,3,2,1,0:T(8,128)(2,1)}, bf16[2,4,4,64,384]{4,3,2,1,0:T(8,128)(2,1)}, u32[]{:S(2)}, u32[]{:S(2)}) collective-permute-start(bf16[2,4,4,64,384]{4,3,2,1,0:T(8,128)(2,1)} %get-tuple-element.7), channel_id=1, source_target_pairs={{0,6},{1,7},{8,14},{9,15},{16,22},{17,23},{24,30},{25,31}} | collective-permute-start | bytes 4718600 | tf_op jit(solution)/shard_map/ppermute | solution.py:21
  183.6 138.3 %collective-permute-start.9 = (bf16[2,4,4,64,384]{4,3,2,1,0:T(8,128)(2,1)}, bf16[2,4,4,64,384]{4,3,2,1,0:T(8,128)(2,1)}, u32[]{:S(2)}, u32[]{:S(2)}) collective-permute-start(bf16[2,4,4,64,384]{4,3,2,1,0:T(8,128)(2,1)} %get-tuple-element.7), channel_id=1, source_target_pairs={{1,0},{2,1},{3,2},{4,3},{5,4},{6,5},{7,6},{9,8},{10,9},{11,10},{12... | collective-permute-start | bytes 4718600 | tf_op jit(solution)/shard_map/ppermute | solution.py:21
  214.8 140.2 %collective-permute-start.10 = (bf16[2,4,4,64,384]{4,3,2,1,0:T(8,128)(2,1)}, bf16[2,4,4,64,384]{4,3,2,1,0:T(8,128)(2,1)}, u32[]{:S(2)}, u32[]{:S(2)}) collective-permute-start(bf16[2,4,4,64,384]{4,3,2,1,0:T(8,128)(2,1)} %get-tuple-element.7), channel_id=1, source_target_pairs={{2,0},{3,1},{4,2},{5,3},{6,4},{7,5},{10,8},{11,9},{12,10},{13,11},... | collective-permute-start | bytes 4718600 | tf_op jit(solution)/shard_map/ppermute | solution.py:21
  248.6 175.3 %collective-permute-start.11 = (bf16[2,4,4,64,384]{4,3,2,1,0:T(8,128)(2,1)}, bf16[2,4,4,64,384]{4,3,2,1,0:T(8,128)(2,1)}, u32[]{:S(2)}, u32[]{:S(2)}) collective-permute-start(bf16[2,4,4,64,384]{4,3,2,1,0:T(8,128)(2,1)} %get-tuple-element.7), channel_id=1, source_target_pairs={{3,0},{4,1},{5,2},{6,3},{7,4},{11,8},{12,9},{13,10},{14,11},{15,12... | collective-permute-start | bytes 4718600 | tf_op jit(solution)/shard_map/ppermute | solution.py:21
  282.3 144.3 %collective-permute-start.12 = (bf16[2,4,4,64,384]{4,3,2,1,0:T(8,128)(2,1)}, bf16[2,4,4,64,384]{4,3,2,1,0:T(8,128)(2,1)}, u32[]{:S(2)}, u32[]{:S(2)}) collective-permute-start(bf16[2,4,4,64,384]{4,3,2,1,0:T(8,128)(2,1)} %get-tuple-element.7), channel_id=1, source_target_pairs={{4,0},{5,1},{6,2},{7,3},{12,8},{13,9},{14,10},{15,11},{20,16},{21,... | collective-permute-start | bytes 4718600 | tf_op jit(solution)/shard_map/ppermute | solution.py:21
  316.0 259.5 %collective-permute-start.13 = (bf16[2,4,4,64,384]{4,3,2,1,0:T(8,128)(2,1)}, bf16[2,4,4,64,384]{4,3,2,1,0:T(8,128)(2,1)}, u32[]{:S(2)}, u32[]{:S(2)}) collective-permute-start(bf16[2,4,4,64,384]{4,3,2,1,0:T(8,128)(2,1)} %get-tuple-element.7), channel_id=1, source_target_pairs={{5,0},{6,1},{7,2},{13,8},{14,9},{15,10},{21,16},{22,17},{23,18},{2... | collective-permute-start | bytes 4718600 | tf_op jit(solution)/shard_map/ppermute | solution.py:21
  321.8 256.4 %collective-permute-start.14 = (bf16[2,4,4,64,384]{4,3,2,1,0:T(8,128)(2,1)}, bf16[2,4,4,64,384]{4,3,2,1,0:T(8,128)(2,1)S(1)}, u32[]{:S(2)}, u32[]{:S(2)}) collective-permute-start(bf16[2,4,4,64,384]{4,3,2,1,0:T(8,128)(2,1)} %get-tuple-element.7), channel_id=1, source_target_pairs={{6,0},{7,1},{14,8},{15,9},{22,16},{23,17},{30,24},{31,25}} | collective-permute-start | bytes 4718600 | tf_op jit(solution)/shard_map/ppermute | solution.py:21
Sparse Core Ops, SparseCore 0:
  708.2 67.5 reduce-scatter.3
